TPU v7x, 32 devices: a whole 2x2x4 slice. The times are simulated.
32 devices in a mesh: section: 4 (over z), dp: 2 (over core), seq: 4 (over y, x).
Axes of the slice: x: 2, y: 2, z: 4, core: 2. Of those that a mesh axis runs over, the one named last changes fastest.
Arguments:
- qkv: bfloat16 [4, 4, 256, 6144], P('section', 'dp', 'seq'), may hold values from -5 to 5
- stream_lengths: int32 [4, 4], P('section'), may hold values from 1 to 192, 256 in all within a row
- doc_lengths: int32 [4, 4, 8], P('section'), may hold values from 1 to 128, 256 in all within a row
- hand_over: int32 [4, 2], P('section'), may hold values from 0 to 1
Outputs:
- handoff: bfloat16 [4, 4, 256, 4096], P('section', 'dp', 'seq')
Inputs may be any that keep to these rules, and one draw needn't show every extreme that they name: `stream_lengths`: each entry is the length of one row; the 4 entries of one section, taken together, sum to 256, and in each section one entry is exactly the most.
All inputs are finite; a program needn't handle non-finite values.
Results may differ from a plain program's by a relative error of at most 0.0013.
Values may be sent and summed in bfloat16 or wider, within the bound.
No kernel may reach another device: no remote copies, remote signals or barrier semaphores. Data moves between devices by JAX's collectives and lax.ppermute only.
A program may use at most 64 MiB of HBM per device.

v0:
```python
import jax
import jax.numpy as jnp
from jax import lax
from jax.sharding import PartitionSpec as P

H = 32
HD = 128
KV_HEADS = 8
D = 4096
RPR = 2


def swapped(block, axis, distance):
    count = lax.axis_size(axis)
    route = []
    for low in range(count):
        high = low | 1 << distance
        if high != low and high < count:
            route += [(low, high), (high, low)]
    return lax.ppermute(block, axis, route)


def passed_along(value, axis, steps):
    count = lax.axis_size(axis)
    pairs = [(source, (source + steps) % count) for source in range(count)]
    return lax.ppermute(value, axis, pairs)


def attend(row_data, row_ids, stream_lengths, doc_ends, seq_count):
    seg_len = row_data.shape[1]
    length = seg_len * seq_count
    heads_dev = H // seq_count
    group_size = H // KV_HEADS
    kv_dev = max(1, heads_dev // group_size)
    copies = max(1, group_size // heads_dev)
    group_local = heads_dev // kv_dev
    q_width = H * HD
    key_value_width = KV_HEADS * HD
    query_send = row_data[..., :q_width].reshape(RPR, seg_len, seq_count, heads_dev * HD)
    key_portion = row_data[..., q_width : q_width + key_value_width]
    value_part = row_data[..., q_width + key_value_width :]
    key_send = jnp.repeat(key_portion.reshape(RPR, seg_len, KV_HEADS, HD), copies, axis=2).reshape(
        RPR, seg_len, seq_count, kv_dev * HD
    )
    value_send = jnp.repeat(value_part.reshape(RPR, seg_len, KV_HEADS, HD), copies, axis=2).reshape(
        RPR, seg_len, seq_count, kv_dev * HD
    )
    query_heads, kv_heads = (
        lax.all_to_all(query_send, "seq", split_axis=2, concat_axis=1, tiled=True),
        lax.all_to_all(
            jnp.concatenate([key_send, value_send], axis=3),
            "seq",
            split_axis=2,
            concat_axis=1,
            tiled=True,
        ),
    )
    key_block = kv_heads[:, :, 0, : kv_dev * HD]
    value_block = kv_heads[:, :, 0, kv_dev * HD :]
    query_tile_rows = query_heads[:, :, 0, :]
    positions = jnp.arange(length, dtype=jnp.int32)
    row_match = (
        jnp.arange(doc_ends.shape[0], dtype=jnp.int32)[None, :] == row_ids[:, None]
    ).astype(jnp.int32)
    ends_rows = jnp.sum(row_match[:, :, None] * doc_ends[None, :, :], axis=1)
    lengths_rows = jnp.sum(row_match * stream_lengths[None, :], axis=1)
    doc_index = jnp.sum(
        (positions[None, :, None] >= ends_rows[:, None, :]).astype(jnp.int32), axis=2
    )
    causal = positions[:, None] >= positions[None, :]
    score_scale = HD ** (-0.5)
    results = []
    for slot_index in range(RPR):
        allowed = causal & (doc_index[slot_index][:, None] == doc_index[slot_index][None, :])
        query_row = query_tile_rows[slot_index].reshape(length, kv_dev, group_local, HD)
        key_row = key_block[slot_index].reshape(length, kv_dev, HD)
        value_row = value_block[slot_index].reshape(length, kv_dev, HD)
        scores = (
            jnp.einsum("qkgd,skd->kgqs", query_row, key_row, preferred_element_type=jnp.float32)
            * score_scale
        )
        row_top = jnp.max(jnp.where(allowed, scores, -jnp.inf), axis=-1, keepdims=True)
        weights = jnp.where(allowed, jnp.exp(scores - row_top), 0.0)
        row_total = jnp.sum(weights, axis=-1)
        rounded = weights.astype(jnp.bfloat16)
        summed = jnp.einsum(
            "kgqs,skd->qkgd", rounded, value_row, preferred_element_type=jnp.float32
        )
        result = summed / jnp.transpose(row_total, (2, 0, 1))[..., None]
        valid = (positions < lengths_rows[slot_index]).astype(jnp.float32)
        result = result * valid[:, None, None, None]
        results.append(result.reshape(length, heads_dev * HD).astype(jnp.bfloat16))
    return jnp.stack(results, axis=0)


def shards(qkv, stream_lengths, doc_lengths, hand_over):
    seq_count = lax.axis_size("seq")
    replica = lax.axis_index("dp")
    partner = jnp.bitwise_xor(replica, 1)
    handed = lax.dynamic_index_in_dim(hand_over[0], replica, 0, keepdims=False)
    partner_handed = lax.dynamic_index_in_dim(hand_over[0], partner, 0, keepdims=False)
    own_rows = qkv[0]
    seg_len = own_rows.shape[1]
    doc_ends = jnp.cumsum(doc_lengths[0], axis=1)
    lengths_all = stream_lengths[0]
    given = lax.dynamic_index_in_dim(own_rows, handed, 0, keepdims=True)
    kept = lax.dynamic_index_in_dim(own_rows, 1 - handed, 0, keepdims=True)
    received = swapped(given, "dp", 0)
    row_ids = jnp.stack([2 * replica + 1 - handed, 2 * partner + partner_handed])
    attention_output = attend(
        jnp.concatenate([kept, received], axis=0), row_ids, lengths_all, doc_ends, seq_count
    )
    grouped = attention_output.reshape(RPR, seq_count, seg_len, attention_output.shape[2])
    tokens = lax.all_to_all(grouped, "seq", split_axis=1, concat_axis=3, tiled=True)
    tokens = passed_along(tokens, "section", 1)
    return tokens.reshape(1, RPR, seg_len, D)


def solution(mesh):
    return jax.shard_map(
        shards,
        mesh=mesh,
        in_specs=(
            P("section", "dp", "seq", None),
            P("section", None),
            P("section", None, None),
            P("section", None),
        ),
        out_specs=P("section", "dp", "seq", None),
        check_vma=False,
    )
```

profile of v0, /device:TPU:0, one launch (start us, length us, event | category | flops | bytes accessed | tf_op | source)
XLA Modules:
  0.0 89.6 jit_solution(12574448168181887721)
XLA Ops:
  0.0 1.4 %constant_dynamic-slice_fusion = (s32[1,1]{1,0:T(1,128)}, s32[1,1]{1,0:T(1,128)}) fusion(s32[1,2]{1,0:T(1,128)} %param.7, s32[]{:T(128)S(6)} %select_n.30, s32[]{:T(128)S(6)} %select_n.27), kind=kLoop, calls=%fused_computation.53 | loop fusion | bytes 24 | tf_op jit(solution)/shard_map/jit(dynamic_index_in_dim)/dynamic_slice | solution.py:101
  4.9 1.5 %dynamic-slice_bitcast_fusion.1 = (bf16[1,64,6144]{2,1,0:T(8,128)(2,1)S(1)}, bf16[1,64,6144]{2,1,0:T(8,128)(2,1)S(1)}) fusion(bf16[1,2,64,6144]{3,2,1,0:T(8,128)(2,1)} %param.4, s32[]{:T(128)S(6)} %select_n.28, s32[]{:T(128)S(6)} %select_n.29), kind=kLoop, calls=%fused_computation.34 | loop fusion | bytes 3145736 | tf_op jit(solution)/shard_map/jit(dynamic_index_in_dim)/dynamic_slice | solution.py:107
  6.3 0.6 collective-permute-start
  8.7 0.7 fusion.38
  9.4 0.6 compare_convert_fusion.1
  10.9 0.9 copy.54
  11.8 4.7 %all-to-all-start = ((bf16[2,64,4,512]{3,1,0,2:T(8,128)(2,1)}), bf16[2,64,4,512]{3,1,0,2:T(8,128)(2,1)S(1)}, u32[]{:S(2)}, u32[]{:S(2)}) async-start(bf16[2,64,4,512]{3,1,0,2:T(8,128)(2,1)} %copy.54), calls=%async_computation | async-start | bytes 1048576 | tf_op jit(solution)/shard_map/all_to_all | solution.py:50
  16.6 1.1 %copy.88 = bf16[2,8,4,8,1024]{4,3,1,0,2:T(8,128)(2,1)} copy(bf16[2,8,4,8,1024]{4,3,2,1,0:T(8,128)(2,1)S(1)} %bitcast.113) | data formatting | bytes 2097152 | tf_op jit(solution)/shard_map/reshape | solution.py:39
  17.7 7.5 %all-to-all-done = bf16[2,64,4,512]{3,1,0,2:T(8,128)(2,1)S(1)} async-done(((bf16[2,64,4,512]{3,1,0,2:T(8,128)(2,1)}), bf16[2,64,4,512]{3,1,0,2:T(8,128)(2,1)S(1)}, u32[]{:S(2)}, u32[]{:S(2)}) %all-to-all-start) | async-done | bytes 524320 | tf_op jit(solution)/shard_map/all_to_all | solution.py:50
  25.2 3.5 %all-to-all-start.1 = ((bf16[2,64,4,1024]{3,1,0,2:T(8,128)(2,1)}), bf16[2,64,4,1024]{3,1,0,2:T(8,128)(2,1)S(1)}, u32[]{:S(2)}, u32[]{:S(2)}) async-start(bf16[2,64,4,1024]{3,1,0,2:T(8,128)(2,1)} %bitcast.111), calls=%async_computation.1 | async-start | bytes 2097152 | tf_op jit(solution)/shard_map/all_to_all | solution.py:49
  28.7 0.7 compare_convert_fusion
  30.2 12.0 %all-to-all-done.1 = bf16[2,64,4,1024]{3,1,0,2:T(8,128)(2,1)S(1)} async-done(((bf16[2,64,4,1024]{3,1,0,2:T(8,128)(2,1)}), bf16[2,64,4,1024]{3,1,0,2:T(8,128)(2,1)S(1)}, u32[]{:S(2)}, u32[]{:S(2)}) %all-to-all-start.1) | async-done | bytes 1048608 | tf_op jit(solution)/shard_map/all_to_all | solution.py:49
  42.2 0.4 reshape_squeeze.20
  42.6 0.5 fusion.26
  43.1 0.9 fusion.40
  44.6 0.4 convert_element_type.63
  45.0 0.4 reshape_squeeze.23
  45.4 0.5 fusion.24
  45.8 0.9 fusion.39
  47.4 0.4 convert_element_type.67
  47.9 16.1 %all_to_all.51 = bf16[2,4,64,1024]{3,2,0,1:T(8,128)(2,1)S(1)} all-to-all(bf16[2,4,64,1024]{3,2,0,1:T(8,128)(2,1)S(1)} %copy.69), channel_id=1, replica_groups=mesh['section'=4,'dp'=2,'seq'=4] {'seq'}, dimensions={1} | all-to-all | bytes 2097152 | tf_op jit(solution)/shard_map/all_to_all | solution.py:114
  64.1 1.6 %collective-permute-start.1 = (bf16[2,1,64,4096]{3,2,0,1:T(8,128)(2,1)S(1)}, bf16[2,1,64,4096]{3,2,0,1:T(8,128)(2,1)S(1)}, u32[]{:S(2)}, u32[]{:S(2)}) collective-permute-start(bf16[2,1,64,4096]{3,2,0,1:T(8,128)(2,1)S(1)} %bitcast.116), channel_id=1, source_target_pairs={{0,8},{8,16},{16,24},{24,0},{1,9},{9,17},{17,25},{25,1},{2,10},{10... | collective-permute-start | bytes 3145736 | tf_op jit(solution)/shard_map/ppermute | solution.py:26
  65.7 22.9 %collective-permute-done.1 = bf16[2,1,64,4096]{3,2,0,1:T(8,128)(2,1)S(1)} collective-permute-done((bf16[2,1,64,4096]{3,2,0,1:T(8,128)(2,1)S(1)}, bf16[2,1,64,4096]{3,2,0,1:T(8,128)(2,1)S(1)}, u32[]{:S(2)}, u32[]{:S(2)}) %collective-permute-start.1) | collective-permute-done | bytes 1048608 | tf_op jit(solution)/shard_map/ppermute | solution.py:26
  88.7 1.0 %copy.90 = bf16[1,2,64,4096]{3,2,1,0:T(8,128)(2,1)} copy(bf16[1,2,64,4096]{3,2,1,0:T(8,128)(2,1)S(1)} %bitcast.117) | data formatting | bytes 2097152
  (33 shorter events, 3.7 us)
Async XLA Ops:
  0.0 7.6 %copy-start = (s32[1,4,8]{2,1,0:T(4,128)S(1)}, s32[1,4,8]{2,1,0:T(4,128)}, u32[]{:S(2)}) copy-start(s32[1,4,8]{2,1,0:T(4,128)} %param.6) | copy-start | bytes 388
  0.0 8.5 %copy-start.1 = (s32[1,4]{1,0:T(1,128)S(1)}, s32[1,4]{1,0:T(1,128)}, u32[]{:S(2)}) copy-start(s32[1,4]{1,0:T(1,128)} %param.5) | copy-start | bytes 52
  6.3 3.9 %collective-permute-start = (bf16[1,64,6144]{2,1,0:T(8,128)(2,1)S(1)}, bf16[1,64,6144]{2,1,0:T(8,128)(2,1)S(1)}, u32[]{:S(2)}, u32[]{:S(2)}) collective-permute-start(bf16[1,64,6144]{2,1,0:T(8,128)(2,1)S(1)} %get-tuple-element.8), channel_id=1, source_target_pairs={{0,4},{4,0},{1,5},{5,1},{2,6},{6,2},{3,7},{7,3},{8,12},{12,8},{9,1... | collective-permute-start | bytes 2359304 | tf_op jit(solution)/shard_map/ppermute | solution.py:20
  11.8 13.4 %all-to-all-start = ((bf16[2,64,4,512]{3,1,0,2:T(8,128)(2,1)}), bf16[2,64,4,512]{3,1,0,2:T(8,128)(2,1)S(1)}, u32[]{:S(2)}, u32[]{:S(2)}) async-start(bf16[2,64,4,512]{3,1,0,2:T(8,128)(2,1)} %copy.54), calls=%async_computation | async-start | bytes 1048576 | tf_op jit(solution)/shard_map/all_to_all | solution.py:50
  25.2 16.9 %all-to-all-start.1 = ((bf16[2,64,4,1024]{3,1,0,2:T(8,128)(2,1)}), bf16[2,64,4,1024]{3,1,0,2:T(8,128)(2,1)S(1)}, u32[]{:S(2)}, u32[]{:S(2)}) async-start(bf16[2,64,4,1024]{3,1,0,2:T(8,128)(2,1)} %bitcast.111), calls=%async_computation.1 | async-start | bytes 2097152 | tf_op jit(solution)/shard_map/all_to_all | solution.py:49
  64.1 24.6 %collective-permute-start.1 = (bf16[2,1,64,4096]{3,2,0,1:T(8,128)(2,1)S(1)}, bf16[2,1,64,4096]{3,2,0,1:T(8,128)(2,1)S(1)}, u32[]{:S(2)}, u32[]{:S(2)}) collective-permute-start(bf16[2,1,64,4096]{3,2,0,1:T(8,128)(2,1)S(1)} %bitcast.116), channel_id=1, source_target_pairs={{0,8},{8,16},{16,24},{24,0},{1,9},{9,17},{17,25},{25,1},{2,10},{10... | collective-permute-start | bytes 3145736 | tf_op jit(solution)/shard_map/ppermute | solution.py:26
where the time goes:
time: 90 us; the launch traced here: 89.6 us
  waiting for transfers between devices  42.4 us (47%)
  blocking collectives  16.1 us (18%)
  starting transfers between devices  10.4 us (12%)
  local copies, waits for them, and re-layouts  9.62 us (11%)
  between operations  5.03 us (6%)
  other arithmetic  4.47 us (5%)
  matrix products  1.61 us (2%)
    ppermute x1, waiting for transfers between devices, passed_along(): return lax.ppermute(value, axis, pairs)  22.9 us
    all_to_all x1, blocking collectives, shards(): lax.all_to_all(grouped, 'seq', split_axis=1, concat_axis=3, tiled=True)  16.1 us
    all_to_all x1, waiting for transfers between devices, attend(): lax.all_to_all(query_send, 'seq', split_axis=2, concat_axis=1, tiled=True)  12 us
    all_to_all x1, waiting for transfers between devices, attend(): lax.all_to_all(jnp.concatenate([key_send, value_send], axis=3), 'seq', sp...  7.52 us
    all_to_all x1, starting transfers between devices, attend(): lax.all_to_all(jnp.concatenate([key_send, value_send], axis=3), 'seq', sp...  4.71 us
    all_to_all x1, starting transfers between devices, attend(): lax.all_to_all(query_send, 'seq', split_axis=2, concat_axis=1, tiled=True)  3.52 us
  transfers between devices with their start and end apart: 4, of which 3 were waited for; matrix products, arithmetic and copies ran while one was open for 5% of the time, Pallas kernels for 0%

commit v1 on v0

--- a/solution.py
+++ b/solution.py
@@ -8,6 +8,22 @@
 KV_HEADS = 8
 D = 4096
 RPR = 2
+
+
+def exchange_in_pairs(x, axis, split, join):
+    ways, here = (lax.axis_size(axis), lax.axis_index(axis))
+    width = x.shape[split] // ways
+    shape = list(x.shape)
+    shape[split] = width
+    height = shape[join]
+    shape[join] = height * ways
+    full = jnp.zeros(shape, x.dtype)
+    for mask in range(ways):
+        part = lax.dynamic_slice_in_dim(x, (here ^ mask) * width, width, axis=split)
+        if mask:
+            part = lax.ppermute(part, axis, [(d, d ^ mask) for d in range(ways)])
+        full = lax.dynamic_update_slice_in_dim(full, part, (here ^ mask) * height, axis=join)
+    return full
 
 
 def swapped(block, axis, distance):
@@ -46,7 +62,7 @@
         RPR, seg_len, seq_count, kv_dev * HD
     )
     query_heads, kv_heads = (
-        lax.all_to_all(query_send, "seq", split_axis=2, concat_axis=1, tiled=True),
+        exchange_in_pairs(query_send, "seq", 2, 1),
         lax.all_to_all(
             jnp.concatenate([key_send, value_send], axis=3),
             "seq",

time: 90 us -> 105 us (1.17)
  local copies, waits for them, and re-layouts: 9.62 us -> 28.9 us
  waiting for transfers between devices: 42.4 us -> 34.7 us
  matrix products: 1.61 us -> 7.05 us
  other arithmetic: 4.47 us -> 2.52 us
    ppermute x0 -> x3, waiting for transfers between devices: none -> 12.5 us  [exchange_in_pairs(): part = lax.ppermute(part, axis, [(d, d ^ mask) for d in range(ways)])]
    dynamic_update_slice x0 -> x4, local copies, waits for them, and re-layouts: none -> 12.4 us  [exchange_in_pairs(): lax.dynamic_update_slice_in_dim(full, part, (here ^ mask) * height, axis=...]
    all_to_all x1 -> x0, waiting for transfers between devices: 12 us -> none  [attend(): lax.all_to_all(query_send, 'seq', split_axis=2, concat_axis=1, tiled=True)]
    all_to_all x1, waiting for transfers between devices: 7.52 us -> 0.01 us  [attend(): lax.all_to_all(jnp.concatenate([key_send, value_send], axis=3), 'seq', sp...]
    squeeze x0 -> x5, local copies, waits for them, and re-layouts: none -> 4.82 us  [attend(): query_tile_rows = query_heads[:, :, 0, :]]
    ppermute x0 -> x3, starting transfers between devices: none -> 4.04 us  [exchange_in_pairs(): part = lax.ppermute(part, axis, [(d, d ^ mask) for d in range(ways)])]
    sub x0 -> x2, matrix products: none -> 3.97 us  [attend(): weights = jnp.where(allowed, jnp.exp(scores - row_top), 0.0)]
    all_to_all x1 -> x0, starting transfers between devices: 3.52 us -> none  [attend(): lax.all_to_all(query_send, 'seq', split_axis=2, concat_axis=1, tiled=True)]
  transfers between devices with their start and end apart: 4 -> 6, of which waited for: 3 -> 3; matrix products, arithmetic and copies ran while one was open for 5% -> 20% of each run, Pallas kernels for 0% -> 0%
where the time goes in v1:
time: 105 us
  waiting for transfers between devices  34.7 us (33%)
  local copies, waits for them, and re-layouts  28.9 us (28%)
  blocking collectives  16.2 us (15%)
  starting transfers between devices  10.3 us (10%)
  matrix products  7.05 us (7%)
  between operations  5.15 us (5%)
  other arithmetic  2.52 us (2%)
    ppermute x1, waiting for transfers between devices, passed_along(): return lax.ppermute(value, axis, pairs)  22.3 us
    all_to_all x1, blocking collectives, shards(): lax.all_to_all(grouped, 'seq', split_axis=1, concat_axis=3, tiled=True)  16.2 us
    ppermute x3, waiting for transfers between devices, exchange_in_pairs(): part = lax.ppermute(part, axis, [(d, d ^ mask) for d in range(ways)])  12.5 us
    dynamic_update_slice x4, local copies, waits for them, and re-layouts, exchange_in_pairs(): lax.dynamic_update_slice_in_dim(full, part, (here ^ mask) * height, axis=...  12.4 us
    squeeze x5, local copies, waits for them, and re-layouts, attend(): query_tile_rows = query_heads[:, :, 0, :]  4.82 us
    all_to_all x1, starting transfers between devices, attend(): lax.all_to_all(jnp.concatenate([key_send, value_send], axis=3), 'seq', sp...  4.19 us
    ppermute x3, starting transfers between devices, exchange_in_pairs(): part = lax.ppermute(part, axis, [(d, d ^ mask) for d in range(ways)])  4.04 us
    sub x2, matrix products, attend(): weights = jnp.where(allowed, jnp.exp(scores - row_top), 0.0)  3.97 us
  transfers between devices with their start and end apart: 6, of which 3 were waited for; matrix products, arithmetic and copies ran while one was open for 20% of the time, Pallas kernels for 0%

profile of v1, /device:TPU:0, one launch (start us, length us, event | category | flops | bytes accessed | tf_op | source)
XLA Modules:
  0.0 105.0 jit_solution(6270119990654447246)
XLA Ops:
  0.0 1.4 %constant_dynamic-slice_fusion.4 = (s32[1,1]{1,0:T(1,128)}, s32[1,1]{1,0:T(1,128)}) fusion(s32[1,2]{1,0:T(1,128)} %param.7, s32[]{:T(128)S(6)} %select_n.54, s32[]{:T(128)S(6)} %select_n.51), kind=kLoop, calls=%fused_computation.49 | loop fusion | bytes 24 | tf_op jit(solution)/shard_map/jit(dynamic_index_in_dim)/dynamic_slice | solution.py:117
  4.9 1.5 %dynamic-slice_bitcast_fusion.1 = (bf16[1,64,6144]{2,1,0:T(8,128)(2,1)S(1)}, bf16[1,64,6144]{2,1,0:T(8,128)(2,1)S(1)}) fusion(bf16[1,2,64,6144]{3,2,1,0:T(8,128)(2,1)} %param.4, s32[]{:T(128)S(6)} %select_n.52, s32[]{:T(128)S(6)} %select_n.53), kind=kLoop, calls=%fused_computation.33 | loop fusion | bytes 3145736 | tf_op jit(solution)/shard_map/jit(dynamic_index_in_dim)/dynamic_slice | solution.py:123
  11.1 3.1 %constant_dynamic-slice_fusion = (bf16[2,64,1,1024]{3,2,1,0:T(2,128)(2,1)}, bf16[2,64,1,1024]{3,2,1,0:T(2,128)(2,1)}, bf16[2,64,1,1024]{3,2,1,0:T(2,128)(2,1)}, bf16[2,64,1,1024]{3,2,1,0:T(2,128)(2,1)S(1)}) fusion(bf16[2,64,4,1024]{3,2,1,0:T(4,128)(2,1)S(1)} %reshape.99, s32[]{:T(128)S(6)} %select_n.61, s32[]{:T(128)S(6)} %select_n.59, s32[]{:T(128)S(6)} %select_n.57, ...), kind=kLoop, calls=%fused_computation.45 | loop fusion | bytes 2097168 | tf_op jit(solution)/shard_map/dynamic_slice | solution.py:22
  14.3 2.5 %collective-permute-start.1 = (bf16[2,64,1,1024]{3,2,1,0:T(2,128)(2,1)}, bf16[2,64,1,1024]{3,2,1,0:T(2,128)(2,1)}, u32[]{:S(2)}, u32[]{:S(2)}) collective-permute-start(bf16[2,64,1,1024]{3,2,1,0:T(2,128)(2,1)} %get-tuple-element.13), channel_id=1, source_target_pairs={{0,1},{1,0},{2,3},{3,2},{4,5},{5,4},{6,7},{7,6},{8,9},{9,8},{10,11... | collective-permute-start | bytes 786440 | tf_op jit(solution)/shard_map/ppermute | solution.py:24
  16.8 1.5 %collective-permute-start.2 = (bf16[2,64,1,1024]{3,2,1,0:T(2,128)(2,1)}, bf16[2,64,1,1024]{3,2,1,0:T(2,128)(2,1)}, u32[]{:S(2)}, u32[]{:S(2)}) collective-permute-start(bf16[2,64,1,1024]{3,2,1,0:T(2,128)(2,1)} %get-tuple-element.12), channel_id=1, source_target_pairs={{0,2},{1,3},{2,0},{3,1},{4,6},{5,7},{6,4},{7,5},{8,10},{9,11},{10,... | collective-permute-start | bytes 786440 | tf_op jit(solution)/shard_map/ppermute | solution.py:24
  18.5 0.9 copy.63
  19.4 4.2 %all-to-all-start = ((bf16[2,64,4,512]{3,1,0,2:T(8,128)(2,1)}), bf16[2,64,4,512]{3,1,0,2:T(8,128)(2,1)S(1)}, u32[]{:S(2)}, u32[]{:S(2)}) async-start(bf16[2,64,4,512]{3,1,0,2:T(8,128)(2,1)} %copy.63), calls=%async_computation | async-start | bytes 1048576 | tf_op jit(solution)/shard_map/all_to_all | solution.py:66
  25.4 2.5 %dynamic_update_slice.16 = bf16[2,256,1024]{1,2,0:T(8,128)(2,1)S(1)} dynamic-update-slice(bf16[2,256,1024]{1,2,0:T(8,128)(2,1)S(1)} %squeeze.32, bf16[2,64,1024]{1,2,0:T(8,128)(2,1)S(1)} %bitcast.111, s32[]{:T(128)} %constant.42.clone.1, s32[]{:T(128)S(6)} %select_n.56, s32[]{:T(128)} %constant.42.clone.1) | dynamic-update-slice | bytes 524292 | tf_op jit(solution)/shard_map/dynamic_update_slice | solution.py:25
  27.9 2.0 %collective-permute-done.1 = bf16[2,64,1,1024]{3,2,1,0:T(2,128)(2,1)} collective-permute-done((bf16[2,64,1,1024]{3,2,1,0:T(2,128)(2,1)}, bf16[2,64,1,1024]{3,2,1,0:T(2,128)(2,1)}, u32[]{:S(2)}, u32[]{:S(2)}) %collective-permute-start.1) | collective-permute-done | bytes 262176 | tf_op jit(solution)/shard_map/ppermute | solution.py:24
  29.9 1.4 %copy.94 = bf16[2,64,1,1024]{1,3,0,2:T(8,128)(2,1)S(1)} copy(bf16[2,64,1,1024]{3,2,1,0:T(2,128)(2,1)} %collective-permute-done.1) | data formatting | bytes 524288 | tf_op jit(solution)/shard_map/squeeze | solution.py:76
  31.3 4.1 %dynamic_update_slice.17 = bf16[2,256,1024]{1,2,0:T(8,128)(2,1)S(1)} dynamic-update-slice(bf16[2,256,1024]{1,2,0:T(8,128)(2,1)S(1)} %dynamic_update_slice.16, bf16[2,64,1024]{1,2,0:T(8,128)(2,1)S(1)} %bitcast.113, s32[]{:T(128)} %constant.42.clone.1, s32[]{:T(128)S(6)} %select_n.58, s32[]{:T(128)} %constant.42.clone.1) | dynamic-update-slice | bytes 524292 | tf_op jit(solution)/shard_map/dynamic_update_slice | solution.py:25
  35.4 10.5 %collective-permute-done.2 = bf16[2,64,1,1024]{3,2,1,0:T(2,128)(2,1)} collective-permute-done((bf16[2,64,1,1024]{3,2,1,0:T(2,128)(2,1)}, bf16[2,64,1,1024]{3,2,1,0:T(2,128)(2,1)}, u32[]{:S(2)}, u32[]{:S(2)}) %collective-permute-start.2) | collective-permute-done | bytes 262176 | tf_op jit(solution)/shard_map/ppermute | solution.py:24
  45.9 1.4 %copy.95 = bf16[2,64,1,1024]{1,3,0,2:T(8,128)(2,1)S(1)} copy(bf16[2,64,1,1024]{3,2,1,0:T(2,128)(2,1)} %collective-permute-done.2) | data formatting | bytes 524288 | tf_op jit(solution)/shard_map/squeeze | solution.py:76
  47.4 2.1 %dynamic_update_slice.18 = bf16[2,256,1024]{1,2,0:T(8,128)(2,1)S(1)} dynamic-update-slice(bf16[2,256,1024]{1,2,0:T(8,128)(2,1)S(1)} %dynamic_update_slice.17, bf16[2,64,1024]{1,2,0:T(8,128)(2,1)S(1)} %bitcast.114, s32[]{:T(128)} %constant.42.clone.1, s32[]{:T(128)S(6)} %select_n.60, s32[]{:T(128)} %constant.42.clone.1) | dynamic-update-slice | bytes 524292 | tf_op jit(solution)/shard_map/dynamic_update_slice | solution.py:25
  49.5 1.4 %copy.96 = bf16[2,64,1,1024]{1,3,0,2:T(8,128)(2,1)S(1)} copy(bf16[2,64,1,1024]{3,2,1,0:T(2,128)(2,1)} %collective-permute-done.3) | data formatting | bytes 524288 | tf_op jit(solution)/shard_map/squeeze | solution.py:76
  50.9 3.7 %dynamic_update_slice.19 = bf16[2,256,1024]{1,2,0:T(8,128)(2,1)S(1)} dynamic-update-slice(bf16[2,256,1024]{1,2,0:T(8,128)(2,1)S(1)} %dynamic_update_slice.18, bf16[2,64,1024]{1,2,0:T(8,128)(2,1)S(1)} %bitcast.112, s32[]{:T(128)} %constant.42.clone.1, s32[]{:T(128)S(6)} %select_n.62, s32[]{:T(128)} %constant.42.clone.1) | dynamic-update-slice | bytes 524292 | tf_op jit(solution)/shard_map/dynamic_update_slice | solution.py:25
  55.0 2.0 %fusion.39 = (f32[2,4,256]{2,1,0:T(4,128)S(1)}, bf16[2,4,256,256]{2,3,1,0:T(8,128)(2,1)}) fusion(pred[256,256]{0,1:T(8,128)(4,1)S(1)} %fusion.24, bf16[256,2,128,1]{0,2,3,1:T(8,128)(2,1)S(1)} %bitcast.122, bf16[256,2,4,128]{0,3,2,1:T(8,128)(2,1)S(1)} %bitcast.118), kind=kOutput, calls=%fused_computation.65 | convolution fusion | flops 272105728 | bytes 1777664 | tf_op jit(solution)/shard_map/sub | solution.py:99
  57.0 1.5 %fusion.15 = bf16[256,2,4,128]{0,3,2,1:T(8,128)(2,1)S(1)} fusion(bf16[256,2,128,1]{0,2,3,1:T(8,128)(2,1)S(1)} %bitcast.120, bf16[2,4,256,256]{2,3,1,0:T(8,128)(2,1)} %get-tuple-element.26, f32[256]{0:T(256)S(1)} %compare_convert_fusion, f32[256,2,4]{0,2,1:T(4,128)S(1)} %bitcast.127), kind=kOutput, calls=%fused_computation.21 | convolution fusion | flops 135004160 | bytes 1713152 | tf_op jit(solution)/shard_map/kgqs,skd->qkgd/dot_general | solution.py:102
  59.4 2.0 %fusion.40 = (f32[2,4,256]{2,1,0:T(4,128)S(1)}, bf16[2,4,256,256]{2,3,1,0:T(8,128)(2,1)}) fusion(pred[256,256]{0,1:T(8,128)(4,1)S(1)} %fusion.25, bf16[256,2,128,1]{0,2,3,1:T(8,128)(2,1)S(1)} %bitcast.121, bf16[256,2,4,128]{0,3,2,1:T(8,128)(2,1)S(1)} %bitcast.117), kind=kOutput, calls=%fused_computation.66 | convolution fusion | flops 272105728 | bytes 1777664 | tf_op jit(solution)/shard_map/sub | solution.py:99
  61.4 1.5 %fusion.14 = bf16[256,2,4,128]{0,3,2,1:T(8,128)(2,1)S(1)} fusion(bf16[256,2,128,1]{0,2,3,1:T(8,128)(2,1)S(1)} %bitcast.119, bf16[2,4,256,256]{2,3,1,0:T(8,128)(2,1)} %get-tuple-element.28, f32[256]{0:T(256)S(1)} %compare_convert_fusion.1, f32[256,2,4]{0,2,1:T(4,128)S(1)} %bitcast.128), kind=kOutput, calls=%fused_computation.20 | convolution fusion | flops 135004160 | bytes 1713152 | tf_op jit(solution)/shard_map/kgqs,skd->qkgd/dot_general | solution.py:102
  63.9 16.2 %all_to_all.36 = bf16[2,4,64,1024]{3,2,0,1:T(8,128)(2,1)S(1)} all-to-all(bf16[2,4,64,1024]{3,2,0,1:T(8,128)(2,1)S(1)} %copy.81), channel_id=1, replica_groups=mesh['section'=4,'dp'=2,'seq'=4] {'seq'}, dimensions={1} | all-to-all | bytes 2097152 | tf_op jit(solution)/shard_map/all_to_all | solution.py:130
  80.2 1.6 %collective-permute-start.4 = (bf16[2,1,64,4096]{3,2,0,1:T(8,128)(2,1)S(1)}, bf16[2,1,64,4096]{3,2,0,1:T(8,128)(2,1)S(1)}, u32[]{:S(2)}, u32[]{:S(2)}) collective-permute-start(bf16[2,1,64,4096]{3,2,0,1:T(8,128)(2,1)S(1)} %bitcast.115), channel_id=1, source_target_pairs={{0,8},{8,16},{16,24},{24,0},{1,9},{9,17},{17,25},{25,1},{2,10},{10... | collective-permute-start | bytes 3145736 | tf_op jit(solution)/shard_map/ppermute | solution.py:42
  81.7 22.3 %collective-permute-done.4 = bf16[2,1,64,4096]{3,2,0,1:T(8,128)(2,1)S(1)} collective-permute-done((bf16[2,1,64,4096]{3,2,0,1:T(8,128)(2,1)S(1)}, bf16[2,1,64,4096]{3,2,0,1:T(8,128)(2,1)S(1)}, u32[]{:S(2)}, u32[]{:S(2)}) %collective-permute-start.4) | collective-permute-done | bytes 1048608 | tf_op jit(solution)/shard_map/ppermute | solution.py:42
  104.0 1.0 copy.105
  (43 shorter events, 7.5 us)
Async XLA Ops:
  4.9 2.1 %copy-start = (s32[1,4,8]{2,1,0:T(4,128)S(1)}, s32[1,4,8]{2,1,0:T(4,128)}, u32[]{:S(2)}) copy-start(s32[1,4,8]{2,1,0:T(4,128)} %param.6) | copy-start | bytes 388
  4.9 3.9 %copy-start.1 = (s32[1,4]{1,0:T(1,128)S(1)}, s32[1,4]{1,0:T(1,128)}, u32[]{:S(2)}) copy-start(s32[1,4]{1,0:T(1,128)} %param.5) | copy-start | bytes 52
  6.4 3.4 %collective-permute-start = (bf16[1,64,6144]{2,1,0:T(8,128)(2,1)S(1)}, bf16[1,64,6144]{2,1,0:T(8,128)(2,1)S(1)}, u32[]{:S(2)}, u32[]{:S(2)}) collective-permute-start(bf16[1,64,6144]{2,1,0:T(8,128)(2,1)S(1)} %get-tuple-element.8), channel_id=1, source_target_pairs={{0,4},{4,0},{1,5},{5,1},{2,6},{6,2},{3,7},{7,3},{8,12},{12,8},{9,1... | collective-permute-start | bytes 2359304 | tf_op jit(solution)/shard_map/ppermute | solution.py:36
  14.3 15.6 %collective-permute-start.1 = (bf16[2,64,1,1024]{3,2,1,0:T(2,128)(2,1)}, bf16[2,64,1,1024]{3,2,1,0:T(2,128)(2,1)}, u32[]{:S(2)}, u32[]{:S(2)}) collective-permute-start(bf16[2,64,1,1024]{3,2,1,0:T(2,128)(2,1)} %get-tuple-element.13), channel_id=1, source_target_pairs={{0,1},{1,0},{2,3},{3,2},{4,5},{5,4},{6,7},{7,6},{8,9},{9,8},{10,11... | collective-permute-start | bytes 786440 | tf_op jit(solution)/shard_map/ppermute | solution.py:24
  16.8 29.2 %collective-permute-start.2 = (bf16[2,64,1,1024]{3,2,1,0:T(2,128)(2,1)}, bf16[2,64,1,1024]{3,2,1,0:T(2,128)(2,1)}, u32[]{:S(2)}, u32[]{:S(2)}) collective-permute-start(bf16[2,64,1,1024]{3,2,1,0:T(2,128)(2,1)} %get-tuple-element.12), channel_id=1, source_target_pairs={{0,2},{1,3},{2,0},{3,1},{4,6},{5,7},{6,4},{7,5},{8,10},{9,11},{10,... | collective-permute-start | bytes 786440 | tf_op jit(solution)/shard_map/ppermute | solution.py:24
  18.3 31.1 %collective-permute-start.3 = (bf16[2,64,1,1024]{3,2,1,0:T(2,128)(2,1)}, bf16[2,64,1,1024]{3,2,1,0:T(2,128)(2,1)}, u32[]{:S(2)}, u32[]{:S(2)}) collective-permute-start(bf16[2,64,1,1024]{3,2,1,0:T(2,128)(2,1)} %get-tuple-element.11), channel_id=1, source_target_pairs={{0,3},{1,2},{2,1},{3,0},{4,7},{5,6},{6,5},{7,4},{8,11},{9,10},{10,... | collective-permute-start | bytes 786440 | tf_op jit(solution)/shard_map/ppermute | solution.py:24
  19.4 35.3 %all-to-all-start = ((bf16[2,64,4,512]{3,1,0,2:T(8,128)(2,1)}), bf16[2,64,4,512]{3,1,0,2:T(8,128)(2,1)S(1)}, u32[]{:S(2)}, u32[]{:S(2)}) async-start(bf16[2,64,4,512]{3,1,0,2:T(8,128)(2,1)} %copy.63), calls=%async_computation | async-start | bytes 1048576 | tf_op jit(solution)/shard_map/all_to_all | solution.py:66
  80.2 23.8 %collective-permute-start.4 = (bf16[2,1,64,4096]{3,2,0,1:T(8,128)(2,1)S(1)}, bf16[2,1,64,4096]{3,2,0,1:T(8,128)(2,1)S(1)}, u32[]{:S(2)}, u32[]{:S(2)}) collective-permute-start(bf16[2,1,64,4096]{3,2,0,1:T(8,128)(2,1)S(1)} %bitcast.115), channel_id=1, source_target_pairs={{0,8},{8,16},{16,24},{24,0},{1,9},{9,17},{17,25},{25,1},{2,10},{10... | collective-permute-start | bytes 3145736 | tf_op jit(solution)/shard_map/ppermute | solution.py:42
